TPU v7x, 32 devices: a whole 2x2x4 slice. The times are simulated.
32 devices in a mesh: rows: 8 (over z, x), cols: 4 (over y, core).
Axes of the slice: x: 2, y: 2, z: 4, core: 2. Of those that a mesh axis runs over, the one named last changes fastest.
Arguments:
- vectors: bfloat16 [64, 131072], P('cols', 'rows'), may hold values from -110 to 110
- tile_vals: bfloat16 [1536, 256, 256], P('rows'), may hold values from -0.21875 to 0.21875
- tile_row: int32 [8, 192], P('rows'), may hold values from 0 to 63
- tile_src: int32 [8, 192], P('rows'), may hold values from 0 to 191, each once within a row
- send_list: int32 [64, 16], P('rows'), may hold values from 0 to 63
- ritz_matrix: bfloat16 [64, 64], P(None, 'cols'), may hold values from -0.75 to 0.75
Outputs:
- rotated: bfloat16 [64, 131072], P('cols', 'rows')
- gram_matrix: float32 [64, 64], P('cols')
- projected: float32 [64, 64], P('cols')
Inputs may be any that keep to these rules, and one draw needn't show every extreme that they name: Each row of tile_src holds every number once, so that each own or received block is read by exactly one tile.
All inputs are finite; a program needn't handle non-finite values.
Results may differ from a plain program's by a relative error of at most 0.0062.
Values may be sent and summed in bfloat16 or wider, within the bound.
No kernel may reach another device: no remote copies, remote signals or barrier semaphores. Data moves between devices by JAX's collectives and lax.ppermute only.
A program may use at most 128 MiB of HBM per device.

v0:
```python
import jax
import jax.numpy as jnp
from jax import lax
from jax.sharding import PartitionSpec as P


def tile_products(sources, tile_block, row_ids, src_ids, nblocks):
    chosen = jnp.take(sources, src_ids, axis=1)
    products = jnp.einsum("ktc,trc->ktr", chosen, tile_block, preferred_element_type=jnp.float32)
    onehot = (row_ids[None, :] == jnp.arange(nblocks, dtype=jnp.int32)[:, None]).astype(jnp.float32)
    summed = jnp.einsum("bt,ktr->kbr", onehot, products, precision=lax.Precision.HIGHEST)
    return summed.reshape(summed.shape[0], -1)


def apply_operator(vectors, tile_vals, tile_row, tile_src, send_list):
    columns, length = vectors.shape
    tile_side = tile_vals.shape[1]
    nblocks = length // tile_side
    blocked = vectors.reshape(columns, nblocks, tile_side)
    outgoing = jnp.take(blocked, send_list.reshape(-1), axis=1)
    incoming = lax.all_to_all(outgoing, "rows", split_axis=1, concat_axis=1, tiled=True)
    row_ids = tile_row.reshape(-1)
    src_ids = tile_src.reshape(-1)
    sources = jnp.concatenate([blocked, incoming], axis=1)
    return tile_products(sources, tile_vals, row_ids, src_ids, nblocks)


def contract_nodes(left_side, right_side):
    return lax.dot_general(
        left_side, right_side, (((1,), (1,)), ((), ())), preferred_element_type=jnp.float32
    )


def body(vectors, tile_vals, tile_row, tile_src, send_list, ritz_matrix):
    first_pass = apply_operator(vectors, tile_vals, tile_row, tile_src, send_list).astype(
        jnp.bfloat16
    )
    second = apply_operator(first_pass, tile_vals, tile_row, tile_src, send_list)
    filtered = (2.0 * second - vectors.astype(jnp.float32)).astype(jnp.bfloat16)
    total_nodes = vectors.shape[1] * lax.axis_size("rows")
    operated = apply_operator(filtered, tile_vals, tile_row, tile_src, send_list).astype(
        jnp.bfloat16
    )
    portion = lax.all_gather(filtered, "cols", axis=0, tiled=True)
    gram_piece = contract_nodes(filtered, portion)
    proj_piece = contract_nodes(operated, portion)
    turned = lax.dot_general(
        ritz_matrix, portion, (((0,), (0,)), ((), ())), preferred_element_type=jnp.float32
    )
    gram_total, proj_total = lax.psum((gram_piece, proj_piece), "rows")
    gram_matrix = gram_total / total_nodes
    projected = proj_total / total_nodes
    rotated = turned.astype(jnp.bfloat16)
    return (rotated, gram_matrix, projected)


def solution(mesh):
    return jax.shard_map(
        body,
        mesh=mesh,
        in_specs=(
            P("cols", "rows"),
            P("rows", None, None),
            P("rows", None),
            P("rows", None),
            P("rows", None),
            P(None, "cols"),
        ),
        out_specs=(P("cols", "rows"), P("cols", None), P("cols", None)),
        check_vma=False,
    )
```

profile of v0, /device:TPU:0, one launch (start us, length us, event | category | flops | bytes accessed | tf_op | source)
XLA Modules:
  0.0 207.6 jit_solution(13215640300237485455)
XLA Ops:
  7.2 0.8 reshape.40
  8.0 1.1 copy.41
  9.1 0.6 gather_fusion
  9.7 1.2 select_bitcast_fusion.2
  10.9 7.4 %all-to-all-start = ((bf16[16,128,256]{2,0,1:T(8,128)(2,1)}), bf16[16,128,256]{2,0,1:T(8,128)(2,1)S(1)}, u32[]{:S(2)}, u32[]{:S(2)}) async-start(bf16[16,128,256]{2,0,1:T(8,128)(2,1)} %select_bitcast_fusion.2), calls=%async_computation | async-start | bytes 2097152 | tf_op jit(solution)/shard_map/all_to_all | solution.py:21
  18.4 25.7 %all-to-all-done = bf16[16,128,256]{2,0,1:T(8,128)(2,1)S(1)} async-done(((bf16[16,128,256]{2,0,1:T(8,128)(2,1)}), bf16[16,128,256]{2,0,1:T(8,128)(2,1)S(1)}, u32[]{:S(2)}, u32[]{:S(2)}) %all-to-all-start) | async-done | bytes 1048608 | tf_op jit(solution)/shard_map/all_to_all | solution.py:21
  44.2 2.0 gather_fusion.1
  46.3 12.0 %convolution_bitcast_fusion.2 = f32[16,192,256]{2,0,1:T(8,128)S(1)} fusion(bf16[192,256,256]{2,1,0:T(8,128)(2,1)} %param.11, bf16[192,16,256]{2,1,0:T(8,128)(2,1)} %gather_fusion.1, pred[192]{0:T(512)(128)(4,1)S(1)} %compare_and_fusion), kind=kOutput, calls=%fused_computation.16 | convolution fusion | flops 403439616 | bytes 29884608 | tf_op jit(solution)/shard_map/ktc,trc->ktr/dot_general | solution.py:9
  58.3 3.2 %fusion.25 = bf16[16,64,256]{2,1,0:T(8,128)(2,1)S(1)} fusion(f32[16,192,256]{2,0,1:T(8,128)S(1)} %convolution_bitcast_fusion.2, s32[192]{0:T(256)S(1)} %bitcast.65), kind=kOutput, calls=%fused_computation.32 | convolution fusion | flops 604254208 | bytes 3670784 | tf_op jit(solution)/shard_map/bt,ktr->kbr/dot_general | solution.py:11
  61.5 0.3 copy.15
  61.8 0.6 gather_fusion.2
  62.6 29.3 %all_to_all.15 = bf16[16,128,256]{2,0,1:T(8,128)(2,1)S(1)} all-to-all(bf16[16,128,256]{2,0,1:T(8,128)(2,1)S(1)} %select_bitcast_fusion.1), channel_id=1, replica_groups=mesh['rows'=8,'cols'=4] {'rows'}, dimensions={1} | all-to-all | bytes 2097152 | tf_op jit(solution)/shard_map/all_to_all | solution.py:21
  92.1 2.0 gather_fusion.3
  94.1 12.0 %convolution_bitcast_fusion.1 = f32[16,192,256]{2,0,1:T(8,128)S(1)} fusion(bf16[192,256,256]{2,1,0:T(8,128)(2,1)} %param.11, bf16[192,16,256]{2,1,0:T(8,128)(2,1)} %gather_fusion.3, pred[192]{0:T(512)(128)(4,1)S(1)} %compare_and_fusion), kind=kOutput, calls=%fused_computation.15 | convolution fusion | flops 403439616 | bytes 29884608 | tf_op jit(solution)/shard_map/ktc,trc->ktr/dot_general | solution.py:9
  106.1 3.2 %fusion.16 = f32[16,256,64]{1,2,0:T(8,128)S(1)} fusion(f32[16,192,256]{2,0,1:T(8,128)S(1)} %convolution_bitcast_fusion.1, s32[192]{0:T(256)S(1)} %bitcast.66), kind=kOutput, calls=%fused_computation.29 | convolution fusion | flops 604254208 | bytes 4195072 | tf_op jit(solution)/shard_map/bt,ktr->kbr/dot_general | solution.py:11
  109.3 0.6 copy.22
  109.9 0.4 copy-done.3
  110.5 0.6 gather_fusion.4
  111.2 1.2 select_bitcast_fusion
  112.4 4.2 %all-to-all-start.2 = ((bf16[16,128,256]{2,0,1:T(8,128)(2,1)}), bf16[16,128,256]{2,0,1:T(8,128)(2,1)}, u32[]{:S(2)}, u32[]{:S(2)}) async-start(bf16[16,128,256]{2,0,1:T(8,128)(2,1)} %select_bitcast_fusion), calls=%async_computation.2 | async-start | bytes 2097152 | tf_op jit(solution)/shard_map/all_to_all | solution.py:21
  117.0 0.5 all-gather.2.cloned.1.call-update
  117.4 24.4 %all-to-all-done.2 = bf16[16,128,256]{2,0,1:T(8,128)(2,1)} async-done(((bf16[16,128,256]{2,0,1:T(8,128)(2,1)}), bf16[16,128,256]{2,0,1:T(8,128)(2,1)}, u32[]{:S(2)}, u32[]{:S(2)}) %all-to-all-start.2) | async-done | bytes 1048608 | tf_op jit(solution)/shard_map/all_to_all | solution.py:21
  141.8 1.4 pad_maximum_fusion.2
  143.2 2.0 gather_fusion.5
  145.2 12.0 %convolution_bitcast_fusion = f32[16,192,256]{2,0,1:T(8,128)S(1)} fusion(bf16[192,256,256]{2,1,0:T(8,128)(2,1)} %param.11, bf16[192,16,256]{2,1,0:T(8,128)(2,1)} %gather_fusion.5, pred[192]{0:T(512)(128)(4,1)S(1)} %compare_and_fusion), kind=kOutput, calls=%fused_computation.14 | convolution fusion | flops 403439616 | bytes 29884608 | tf_op jit(solution)/shard_map/ktc,trc->ktr/dot_general | solution.py:9
  157.2 3.2 %fusion.22 = bf16[16,256,64]{1,2,0:T(8,128)(2,1)S(1)} fusion(f32[16,192,256]{2,0,1:T(8,128)S(1)} %convolution_bitcast_fusion, s32[192]{0:T(256)S(1)} %bitcast.67), kind=kOutput, calls=%fused_computation.31 | convolution fusion | flops 604254208 | bytes 3670784 | tf_op jit(solution)/shard_map/bt,ktr->kbr/dot_general | solution.py:11
  160.4 0.3 copy.23
  160.7 2.5 %fusion.41 = f32[16,64]{1,0:T(8,128)S(1)} fusion(bf16[16,16384]{1,0:T(8,128)(2,1)} %copy-done.2, bf16[64,16384]{1,0:T(8,128)(2,1)} %all-gather.2.cloned.1.call-done), kind=kOutput, calls=%fused_computation.58 | convolution fusion | flops 33554432 | bytes 2625536 | tf_op jit(solution)/shard_map/dot_general | solution.py:29
  163.3 0.7 fusion.42
  163.9 35.0 %all-reduce = (f32[16,64]{1,0:T(8,128)S(1)}, f32[16,64]{1,0:T(8,128)S(1)}) all-reduce(f32[16,64]{1,0:T(8,128)S(1)} %fusion.41, f32[16,64]{1,0:T(8,128)S(1)} %fusion.42), channel_id=1, replica_groups=mesh['rows'=8,'cols'=4] {'rows'}, use_global_device_ids=true, to_apply=%region_0.3 | all-reduce | flops 2048 | bytes 16384 | tf_op jit(solution)/shard_map/psum | solution.py:50
  198.9 0.6 broadcast_multiply_fusion
  199.5 1.2 fusion
  (24 shorter events, 1.0 us)
Async XLA Ops:
  7.2 192.4 %copy-start = (bf16[64,16]{0,1:T(8,128)(2,1)S(1)}, bf16[64,16]{0,1:T(8,128)(2,1)}, u32[]{:S(2)}) copy-start(bf16[64,16]{0,1:T(8,128)(2,1)} %param.15) | copy-start | bytes 6148
  10.9 7.4 %copy-start.5 = (s32[1,192]{1,0:T(1,128)S(1)}, s32[1,192]{1,0:T(1,128)}, u32[]{:S(2)}) copy-start(s32[1,192]{1,0:T(1,128)} %param.13) | copy-start | bytes 2308
  10.9 33.2 %all-to-all-start = ((bf16[16,128,256]{2,0,1:T(8,128)(2,1)}), bf16[16,128,256]{2,0,1:T(8,128)(2,1)S(1)}, u32[]{:S(2)}, u32[]{:S(2)}) async-start(bf16[16,128,256]{2,0,1:T(8,128)(2,1)} %select_bitcast_fusion.2), calls=%async_computation | async-start | bytes 2097152 | tf_op jit(solution)/shard_map/all_to_all | solution.py:21
  46.3 12.1 %copy-start.4 = (s32[1,192]{1,0:T(1,128)S(1)}, s32[1,192]{1,0:T(1,128)}, u32[]{:S(2)}) copy-start(s32[1,192]{1,0:T(1,128)} %param.12) | copy-start | bytes 2308
  109.3 1.0 copy-start.3
  110.4 0.8 copy-start.2
  112.4 29.4 %all-to-all-start.2 = ((bf16[16,128,256]{2,0,1:T(8,128)(2,1)}), bf16[16,128,256]{2,0,1:T(8,128)(2,1)}, u32[]{:S(2)}, u32[]{:S(2)}) async-start(bf16[16,128,256]{2,0,1:T(8,128)(2,1)} %select_bitcast_fusion), calls=%async_computation.2 | async-start | bytes 2097152 | tf_op jit(solution)/shard_map/all_to_all | solution.py:21
  116.7 44.0 %all-gather.2.cloned.1.call-start = ((), (), s32[]{:S(2)}) async-start(), calls=%async_computation.3 | async-start | bytes 2621440 | tf_op jit(solution)/shard_map/all_gather | solution.py:44
  160.7 2.6 %copy-start.1 = (bf16[64,16384]{1,0:T(8,128)(2,1)S(1)}, bf16[64,16384]{1,0:T(8,128)(2,1)}, u32[]{:S(2)}) copy-start(bf16[64,16384]{1,0:T(8,128)(2,1)} %all-gather.2.cloned.1.call-done) | copy-start | bytes 6291460
Sparse Core Ops, SparseCore 0:
  119.6 23.8 all-gather.1
where the time goes:
time: 208 us
  blocking collectives  64.2 us (31%)
  waiting for transfers between devices  50.6 us (24%)
  matrix products  50 us (24%)
  between operations  14.2 us (7%)
  starting transfers between devices  11.9 us (6%)
  local copies, waits for them, and re-layouts  11.7 us (6%)
  other arithmetic  4.96 us (2%)
    all_to_all x2, waiting for transfers between devices, apply_operator(): lax.all_to_all(outgoing, 'rows', split_axis=1, concat_axis=1, tiled=True)  50.1 us
    dot_general x3, matrix products, tile_products(): jnp.einsum('ktc,trc->ktr', chosen, tile_block, preferred_element_type=jnp...  36.1 us
    psum x1, blocking collectives, body(): gram_total, proj_total = lax.psum((gram_piece, proj_piece), 'rows')  35 us
    all_to_all x1, blocking collectives, apply_operator(): lax.all_to_all(outgoing, 'rows', split_axis=1, concat_axis=1, tiled=True)  29.3 us
    all_to_all x2, starting transfers between devices, apply_operator(): lax.all_to_all(outgoing, 'rows', split_axis=1, concat_axis=1, tiled=True)  11.6 us
    dot_general x3, matrix products, tile_products(): jnp.einsum('bt,ktr->kbr', onehot, products, precision=lax.Precision.HIGHEST)  9.49 us
    gather x3, local copies, waits for them, and re-layouts, tile_products(): chosen = jnp.take(sources, src_ids, axis=1)  6.1 us
  transfers between devices with their start and end apart: 3, of which 2 were waited for; matrix products, arithmetic and copies ran while one was open for 9% of the time, Pallas kernels for 0%

commit v1 on v0

--- a/solution.py
+++ b/solution.py
@@ -2,6 +2,27 @@
 import jax.numpy as jnp
 from jax import lax
 from jax.sharding import PartitionSpec as P
+
+
+def handle_rates_in(target, along_dim, array_here):
+    carry_out = target.shape
+    block_now = target.reshape(
+        *carry_out[:along_dim],
+        array_here,
+        carry_out[along_dim] // array_here,
+        *carry_out[along_dim + 1 :]
+    )
+    t_next = jnp.moveaxis(block_now, along_dim, 0)
+    return t_next
+
+
+def note_signs_over_axis(v0, dim_no):
+    v0 = jnp.moveaxis(v0, 0, dim_no)
+    step_out = v0.shape
+    clean = v0.reshape(
+        *step_out[:dim_no], step_out[dim_no] * step_out[dim_no + 1], *step_out[dim_no + 2 :]
+    )
+    return clean
 
 
 def tile_products(sources, tile_block, row_ids, src_ids, nblocks):
@@ -13,12 +34,30 @@
 
 
 def apply_operator(vectors, tile_vals, tile_row, tile_src, send_list):
+
+    def form_islands(values, row_axis, buf, panel):
+        all_rows = jax.lax.psum(1, row_axis)
+        v_now = jax.lax.axis_index(row_axis)
+        found_now, piece_next = (all_rows, v_now)
+        newest = handle_rates_in(values, buf, found_now)
+        vals = [newest[piece_next]]
+        for c in range(1, found_now):
+            p_next = newest[piece_next ^ c]
+            x_next = jax.lax.ppermute(
+                p_next, row_axis, [(dev_j, dev_j ^ c) for dev_j in range(found_now)]
+            )
+            vals.append(x_next)
+        w1 = jnp.stack(vals)
+        newest = w1[piece_next ^ jnp.arange(found_now)]
+        current_value = note_signs_over_axis(newest, panel)
+        return current_value
+
     columns, length = vectors.shape
     tile_side = tile_vals.shape[1]
     nblocks = length // tile_side
     blocked = vectors.reshape(columns, nblocks, tile_side)
     outgoing = jnp.take(blocked, send_list.reshape(-1), axis=1)
-    incoming = lax.all_to_all(outgoing, "rows", split_axis=1, concat_axis=1, tiled=True)
+    incoming = form_islands(outgoing, "rows", 1, 1)
     row_ids = tile_row.reshape(-1)
     src_ids = tile_src.reshape(-1)
     sources = jnp.concatenate([blocked, incoming], axis=1)

time: 208 us -> 206 us (level)
  starting transfers between devices: 11.9 us -> 43.5 us
  blocking collectives: 64.2 us -> 36.9 us
  waiting for transfers between devices: 50.6 us -> 38.7 us
  local copies, waits for them, and re-layouts: 11.7 us -> 18.1 us
    all_to_all x2 -> x0, waiting for transfers between devices: 50.1 us -> none  [apply_operator(): lax.all_to_all(outgoing, 'rows', split_axis=1, concat_axis=1, tiled=True)]
    ppermute x0 -> x21, starting transfers between devices: none -> 43.5 us  [form_islands(): jax.lax.ppermute(p_next, row_axis, [(dev_j, dev_j ^ c) for dev_j in range...]
    ppermute x0 -> x21, waiting for transfers between devices: none -> 38.6 us  [form_islands(): jax.lax.ppermute(p_next, row_axis, [(dev_j, dev_j ^ c) for dev_j in range...]
    all_to_all x1 -> x0, blocking collectives: 29.3 us -> none  [apply_operator(): lax.all_to_all(outgoing, 'rows', split_axis=1, concat_axis=1, tiled=True)]
    all_to_all x2 -> x0, starting transfers between devices: 11.6 us -> none  [apply_operator(): lax.all_to_all(outgoing, 'rows', split_axis=1, concat_axis=1, tiled=True)]
  transfers between devices with their start and end apart: 3 -> 22, of which waited for: 2 -> 7; matrix products, arithmetic and copies ran while one was open for 9% -> 11% of each run, Pallas kernels for 0% -> 0%
where the time goes in v1:
time: 206 us
  matrix products  50.4 us (24%)
  starting transfers between devices  43.5 us (21%)
  waiting for transfers between devices  38.7 us (19%)
  blocking collectives  36.9 us (18%)
  local copies, waits for them, and re-layouts  18.1 us (9%)
  between operations  14.7 us (7%)
  other arithmetic  3.84 us (2%)
    ppermute x21, starting transfers between devices, form_islands(): jax.lax.ppermute(p_next, row_axis, [(dev_j, dev_j ^ c) for dev_j in range...  43.5 us
    ppermute x21, waiting for transfers between devices, form_islands(): jax.lax.ppermute(p_next, row_axis, [(dev_j, dev_j ^ c) for dev_j in range...  38.6 us
    psum x1, blocking collectives, body(): gram_total, proj_total = lax.psum((gram_piece, proj_piece), 'rows')  36.9 us
    dot_general x3, matrix products, tile_products(): jnp.einsum('ktc,trc->ktr', chosen, tile_block, preferred_element_type=jnp...  36.5 us
    dot_general x3, matrix products, tile_products(): jnp.einsum('bt,ktr->kbr', onehot, products, precision=lax.Precision.HIGHEST)  9.46 us
    gather x3, local copies, waits for them, and re-layouts, tile_products(): chosen = jnp.take(sources, src_ids, axis=1)  6.14 us
  transfers between devices with their start and end apart: 22, of which 7 were waited for; matrix products, arithmetic and copies ran while one was open for 11% of the time, Pallas kernels for 0%

profile of v1, /device:TPU:0, one launch (start us, length us, event | category | flops | bytes accessed | tf_op | source)
XLA Modules:
  0.0 206.1 jit_solution(7198128277832804915)
XLA Ops:
  10.9 3.0 %collective-permute-start = (bf16[16,16,256]{2,1,0:T(8,128)(2,1)S(1)}, bf16[16,16,256]{2,1,0:T(8,128)(2,1)S(1)}, u32[]{:S(2)}, u32[]{:S(2)}) collective-permute-start(bf16[16,16,256]{2,1,0:T(8,128)(2,1)S(1)} %bitcast.212), channel_id=1, source_target_pairs={{0,4},{4,0},{8,12},{12,8},{16,20},{20,16},{24,28},{28,24},{1,5},{5... | collective-permute-start | bytes 393224 | tf_op jit(solution)/shard_map/ppermute | solution.py:46
  14.0 1.6 collective-permute-start.1
  15.8 3.1 %collective-permute-start.3 = (bf16[16,16,256]{2,1,0:T(8,128)(2,1)S(1)}, bf16[16,16,256]{2,1,0:T(8,128)(2,1)S(1)}, u32[]{:S(2)}, u32[]{:S(2)}) collective-permute-start(bf16[16,16,256]{2,1,0:T(8,128)(2,1)S(1)} %bitcast.200), channel_id=1, source_target_pairs={{0,16},{4,20},{8,24},{12,28},{16,0},{20,4},{24,8},{28,12},{1,17},{... | collective-permute-start | bytes 393224 | tf_op jit(solution)/shard_map/ppermute | solution.py:46
  18.9 1.3 collective-permute-start.4
  20.4 3.7 %collective-permute-start.5 = (bf16[16,16,256]{2,1,0:T(8,128)(2,1)S(1)}, bf16[16,16,256]{2,1,0:T(8,128)(2,1)S(1)}, u32[]{:S(2)}, u32[]{:S(2)}) collective-permute-start(bf16[16,16,256]{2,1,0:T(8,128)(2,1)S(1)} %bitcast.202), channel_id=1, source_target_pairs={{0,24},{4,28},{8,16},{12,20},{16,8},{20,12},{24,0},{28,4},{1,25},{... | collective-permute-start | bytes 393224 | tf_op jit(solution)/shard_map/ppermute | solution.py:46
  25.2 12.9 %collective-permute-done.4 = bf16[16,16,256]{2,1,0:T(8,128)(2,1)S(1)} collective-permute-done((bf16[16,16,256]{2,1,0:T(8,128)(2,1)S(1)}, bf16[16,16,256]{2,1,0:T(8,128)(2,1)S(1)}, u32[]{:S(2)}, u32[]{:S(2)}) %collective-permute-start.4) | collective-permute-done | bytes 131104 | tf_op jit(solution)/shard_map/ppermute | solution.py:46
  39.6 2.1 %gather_fusion.4 = bf16[192,16,256]{2,1,0:T(8,128)(2,1)} fusion(bf16[16,192,256]{2,0,1:T(8,128)(2,1)S(1)} %pad_maximum_fusion, s32[1024]{0:T(1024)S(1)} %get-tuple-element.31), kind=kCustom, calls=%fused_computation.1.clone | custom fusion | bytes 3146496 | tf_op jit(solution)/shard_map/jit(_take)/gather | solution.py:29
  41.7 12.0 %convolution_bitcast_fusion.2 = f32[16,192,256]{2,0,1:T(8,128)S(1)} fusion(bf16[192,256,256]{2,1,0:T(8,128)(2,1)} %param.11, bf16[192,16,256]{2,1,0:T(8,128)(2,1)} %gather_fusion.4, pred[192]{0:T(512)(128)(4,1)S(1)} %compare_and_fusion), kind=kOutput, calls=%fused_computation.19 | convolution fusion | flops 403439616 | bytes 29884608 | tf_op jit(solution)/shard_map/ktc,trc->ktr/dot_general | solution.py:30
  53.8 3.1 %fusion.25 = bf16[16,64,256]{2,1,0:T(8,128)(2,1)S(1)} fusion(f32[16,192,256]{2,0,1:T(8,128)S(1)} %convolution_bitcast_fusion.2, s32[192]{0:T(256)S(1)} %bitcast.217), kind=kOutput, calls=%fused_computation.35 | convolution fusion | flops 604254208 | bytes 3670784 | tf_op jit(solution)/shard_map/bt,ktr->kbr/dot_general | solution.py:32
  59.1 4.9 %collective-permute-start.8 = (bf16[16,16,256]{2,1,0:T(8,128)(2,1)S(1)}, bf16[16,16,256]{2,1,0:T(8,128)(2,1)S(1)}, u32[]{:S(2)}, u32[]{:S(2)}) collective-permute-start(bf16[16,16,256]{2,1,0:T(8,128)(2,1)S(1)} %bitcast.213), channel_id=1, source_target_pairs={{0,8},{4,12},{8,0},{12,4},{16,24},{20,28},{24,16},{28,20},{1,9},{5... | collective-permute-start | bytes 393224 | tf_op jit(solution)/shard_map/ppermute | solution.py:46
  65.2 3.6 %collective-permute-start.10 = (bf16[16,16,256]{2,1,0:T(8,128)(2,1)S(1)}, bf16[16,16,256]{2,1,0:T(8,128)(2,1)S(1)}, u32[]{:S(2)}, u32[]{:S(2)}) collective-permute-start(bf16[16,16,256]{2,1,0:T(8,128)(2,1)S(1)} %bitcast.207), channel_id=1, source_target_pairs={{0,16},{4,20},{8,24},{12,28},{16,0},{20,4},{24,8},{28,12},{1,17},{... | collective-permute-start | bytes 393224 | tf_op jit(solution)/shard_map/ppermute | solution.py:46
  69.1 2.4 %collective-permute-start.12 = (bf16[16,16,256]{2,1,0:T(8,128)(2,1)S(1)}, bf16[16,16,256]{2,1,0:T(8,128)(2,1)S(1)}, u32[]{:S(2)}, u32[]{:S(2)}) collective-permute-start(bf16[16,16,256]{2,1,0:T(8,128)(2,1)S(1)} %bitcast.203), channel_id=1, source_target_pairs={{0,24},{4,28},{8,16},{12,20},{16,8},{20,12},{24,0},{28,4},{1,25},{... | collective-permute-start | bytes 393224 | tf_op jit(solution)/shard_map/ppermute | solution.py:46
  71.5 2.5 %collective-permute-start.13 = (bf16[16,16,256]{2,1,0:T(8,128)(2,1)S(1)}, bf16[16,16,256]{2,1,0:T(8,128)(2,1)S(1)}, u32[]{:S(2)}, u32[]{:S(2)}) collective-permute-start(bf16[16,16,256]{2,1,0:T(8,128)(2,1)S(1)} %bitcast.196), channel_id=1, source_target_pairs={{0,28},{4,24},{8,20},{12,16},{16,12},{20,8},{24,4},{28,0},{1,29},{... | collective-permute-start | bytes 393224 | tf_op jit(solution)/shard_map/ppermute | solution.py:46
  74.1 9.6 %collective-permute-done.10 = bf16[16,16,256]{2,1,0:T(8,128)(2,1)S(1)} collective-permute-done((bf16[16,16,256]{2,1,0:T(8,128)(2,1)S(1)}, bf16[16,16,256]{2,1,0:T(8,128)(2,1)S(1)}, u32[]{:S(2)}, u32[]{:S(2)}) %collective-permute-start.10) | collective-permute-done | bytes 131104 | tf_op jit(solution)/shard_map/ppermute | solution.py:46
  83.8 3.0 %collective-permute-done.11 = bf16[16,16,256]{2,1,0:T(8,128)(2,1)S(1)} collective-permute-done((bf16[16,16,256]{2,1,0:T(8,128)(2,1)S(1)}, bf16[16,16,256]{2,1,0:T(8,128)(2,1)S(1)}, u32[]{:S(2)}, u32[]{:S(2)}) %collective-permute-start.11) | collective-permute-done | bytes 131104 | tf_op jit(solution)/shard_map/ppermute | solution.py:46
  88.3 2.1 %gather_fusion.6 = bf16[192,16,256]{2,1,0:T(8,128)(2,1)} fusion(bf16[16,192,256]{2,0,1:T(8,128)(2,1)S(1)} %pad_maximum_fusion.1, s32[1024]{0:T(1024)S(1)} %get-tuple-element.31), kind=kCustom, calls=%fused_computation.4.clone | custom fusion | bytes 3146496 | tf_op jit(solution)/shard_map/jit(_take)/gather | solution.py:29
  90.4 12.2 %convolution_bitcast_fusion.1 = f32[16,192,256]{2,0,1:T(8,128)S(1)} fusion(bf16[192,256,256]{2,1,0:T(8,128)(2,1)} %param.11, bf16[192,16,256]{2,1,0:T(8,128)(2,1)} %gather_fusion.6, pred[192]{0:T(512)(128)(4,1)S(1)} %compare_and_fusion), kind=kOutput, calls=%fused_computation.18 | convolution fusion | flops 403439616 | bytes 29884608 | tf_op jit(solution)/shard_map/ktc,trc->ktr/dot_general | solution.py:30
  102.6 3.2 %fusion.16 = f32[16,256,64]{1,2,0:T(8,128)S(1)} fusion(f32[16,192,256]{2,0,1:T(8,128)S(1)} %convolution_bitcast_fusion.1, s32[192]{0:T(256)S(1)} %bitcast.218), kind=kOutput, calls=%fused_computation.32 | convolution fusion | flops 604254208 | bytes 4195072 | tf_op jit(solution)/shard_map/bt,ktr->kbr/dot_general | solution.py:32
  107.7 1.1 copy.97
  109.8 1.3 collective-permute-start.14
  111.2 4.6 %collective-permute-start.15 = (bf16[16,16,256]{2,1,0:T(8,128)(2,1)S(1)}, bf16[16,16,256]{2,1,0:T(8,128)(2,1)S(1)}, u32[]{:S(2)}, u32[]{:S(2)}) collective-permute-start(bf16[16,16,256]{2,1,0:T(8,128)(2,1)S(1)} %bitcast.214), channel_id=1, source_target_pairs={{0,8},{4,12},{8,0},{12,4},{16,24},{20,28},{24,16},{28,20},{1,9},{5... | collective-permute-start | bytes 393224 | tf_op jit(solution)/shard_map/ppermute | solution.py:46
  116.8 2.2 %collective-permute-start.17 = (bf16[16,16,256]{2,1,0:T(8,128)(2,1)S(1)}, bf16[16,16,256]{2,1,0:T(8,128)(2,1)S(1)}, u32[]{:S(2)}, u32[]{:S(2)}) collective-permute-start(bf16[16,16,256]{2,1,0:T(8,128)(2,1)S(1)} %bitcast.208), channel_id=1, source_target_pairs={{0,16},{4,20},{8,24},{12,28},{16,0},{20,4},{24,8},{28,12},{1,17},{... | collective-permute-start | bytes 393224 | tf_op jit(solution)/shard_map/ppermute | solution.py:46
  120.1 2.1 %collective-permute-start.19 = (bf16[16,16,256]{2,1,0:T(8,128)(2,1)S(1)}, bf16[16,16,256]{2,1,0:T(8,128)(2,1)S(1)}, u32[]{:S(2)}, u32[]{:S(2)}) collective-permute-start(bf16[16,16,256]{2,1,0:T(8,128)(2,1)S(1)} %bitcast.204), channel_id=1, source_target_pairs={{0,24},{4,28},{8,16},{12,20},{16,8},{20,12},{24,0},{28,4},{1,25},{... | collective-permute-start | bytes 393224 | tf_op jit(solution)/shard_map/ppermute | solution.py:46
  122.2 2.7 %collective-permute-start.20 = (bf16[16,16,256]{2,1,0:T(8,128)(2,1)S(1)}, bf16[16,16,256]{2,1,0:T(8,128)(2,1)S(1)}, u32[]{:S(2)}, u32[]{:S(2)}) collective-permute-start(bf16[16,16,256]{2,1,0:T(8,128)(2,1)S(1)} %bitcast.197), channel_id=1, source_target_pairs={{0,28},{4,24},{8,20},{12,16},{16,12},{20,8},{24,4},{28,0},{1,29},{... | collective-permute-start | bytes 393224 | tf_op jit(solution)/shard_map/ppermute | solution.py:46
  125.8 9.0 %collective-permute-done.17 = bf16[16,16,256]{2,1,0:T(8,128)(2,1)S(1)} collective-permute-done((bf16[16,16,256]{2,1,0:T(8,128)(2,1)S(1)}, bf16[16,16,256]{2,1,0:T(8,128)(2,1)S(1)}, u32[]{:S(2)}, u32[]{:S(2)}) %collective-permute-start.17) | collective-permute-done | bytes 131104 | tf_op jit(solution)/shard_map/ppermute | solution.py:46
  134.7 2.7 %collective-permute-done.18 = bf16[16,16,256]{2,1,0:T(8,128)(2,1)S(1)} collective-permute-done((bf16[16,16,256]{2,1,0:T(8,128)(2,1)S(1)}, bf16[16,16,256]{2,1,0:T(8,128)(2,1)S(1)}, u32[]{:S(2)}, u32[]{:S(2)}) %collective-permute-start.18) | collective-permute-done | bytes 131104 | tf_op jit(solution)/shard_map/ppermute | solution.py:46
  139.0 2.0 gather_fusion.8
  141.0 12.3 %convolution_bitcast_fusion = f32[16,192,256]{2,0,1:T(8,128)S(1)} fusion(bf16[192,256,256]{2,1,0:T(8,128)(2,1)} %param.11, bf16[192,16,256]{2,1,0:T(8,128)(2,1)} %gather_fusion.8, pred[192]{0:T(512)(128)(4,1)S(1)} %compare_and_fusion), kind=kOutput, calls=%fused_computation.17 | convolution fusion | flops 403439616 | bytes 29884608 | tf_op jit(solution)/shard_map/ktc,trc->ktr/dot_general | solution.py:30
  153.2 3.2 %fusion.22 = bf16[16,256,64]{1,2,0:T(8,128)(2,1)S(1)} fusion(f32[16,192,256]{2,0,1:T(8,128)S(1)} %convolution_bitcast_fusion, s32[192]{0:T(256)S(1)} %bitcast.219), kind=kOutput, calls=%fused_computation.34 | convolution fusion | flops 604254208 | bytes 3670784 | tf_op jit(solution)/shard_map/bt,ktr->kbr/dot_general | solution.py:32
  156.7 2.5 %fusion.42 = f32[16,64]{1,0:T(8,128)S(1)} fusion(bf16[16,16384]{1,0:T(8,128)(2,1)} %subtract_convert_fusion, bf16[64,16384]{1,0:T(8,128)(2,1)} %all-gather.2.cloned.1.call-done), kind=kOutput, calls=%fused_computation.133 | convolution fusion | flops 33554432 | bytes 2625536 | tf_op jit(solution)/shard_map/dot_general | solution.py:68
  159.9 36.9 %all-reduce = (f32[16,64]{1,0:T(8,128)S(1)}, f32[16,64]{1,0:T(8,128)S(1)}) all-reduce(f32[16,64]{1,0:T(8,128)S(1)} %fusion.42, f32[16,64]{1,0:T(8,128)S(1)} %fusion.43), channel_id=1, replica_groups=mesh['rows'=8,'cols'=4] {'rows'}, use_global_device_ids=true, to_apply=%region_0.3 | all-reduce | flops 2048 | bytes 16384 | tf_op jit(solution)/shard_map/psum | solution.py:89
  198.0 1.2 fusion
  (118 shorter events, 21.3 us)
Async XLA Ops:
  7.2 190.9 %copy-start = (bf16[64,16]{0,1:T(8,128)(2,1)S(1)}, bf16[64,16]{0,1:T(8,128)(2,1)}, u32[]{:S(2)}) copy-start(bf16[64,16]{0,1:T(8,128)(2,1)} %param.15) | copy-start | bytes 6148
  7.2 149.5 %all-gather.2.cloned.1.call-start = ((), (), s32[]{:S(2)}) async-start(), calls=%async_computation | async-start | bytes 2621440 | tf_op jit(solution)/shard_map/all_gather | solution.py:83
  10.7 9.5 %copy-start.4 = (s32[1,192]{1,0:T(1,128)S(1)}, s32[1,192]{1,0:T(1,128)}, u32[]{:S(2)}) copy-start(s32[1,192]{1,0:T(1,128)} %param.13) | copy-start | bytes 2308
  10.9 9.5 %collective-permute-start = (bf16[16,16,256]{2,1,0:T(8,128)(2,1)S(1)}, bf16[16,16,256]{2,1,0:T(8,128)(2,1)S(1)}, u32[]{:S(2)}, u32[]{:S(2)}) collective-permute-start(bf16[16,16,256]{2,1,0:T(8,128)(2,1)S(1)} %bitcast.212), channel_id=1, source_target_pairs={{0,4},{4,0},{8,12},{12,8},{16,20},{20,16},{24,28},{28,24},{1,5},{5... | collective-permute-start | bytes 393224 | tf_op jit(solution)/shard_map/ppermute | solution.py:46
  14.0 10.7 %collective-permute-start.1 = (bf16[16,16,256]{2,1,0:T(8,128)(2,1)S(1)}, bf16[16,16,256]{2,1,0:T(8,128)(2,1)S(1)}, u32[]{:S(2)}, u32[]{:S(2)}) collective-permute-start(bf16[16,16,256]{2,1,0:T(8,128)(2,1)S(1)} %bitcast.209), channel_id=1, source_target_pairs={{0,8},{4,12},{8,0},{12,4},{16,24},{20,28},{24,16},{28,20},{1,9},{5... | collective-permute-start | bytes 393224 | tf_op jit(solution)/shard_map/ppermute | solution.py:46
  15.6 9.5 %collective-permute-start.2 = (bf16[16,16,256]{2,1,0:T(8,128)(2,1)S(1)}, bf16[16,16,256]{2,1,0:T(8,128)(2,1)S(1)}, u32[]{:S(2)}, u32[]{:S(2)}) collective-permute-start(bf16[16,16,256]{2,1,0:T(8,128)(2,1)S(1)} %bitcast.201), channel_id=1, source_target_pairs={{0,12},{4,8},{8,4},{12,0},{16,28},{20,24},{24,20},{28,16},{1,13},{... | collective-permute-start | bytes 393224 | tf_op jit(solution)/shard_map/ppermute | solution.py:46
  15.8 9.4 %collective-permute-start.3 = (bf16[16,16,256]{2,1,0:T(8,128)(2,1)S(1)}, bf16[16,16,256]{2,1,0:T(8,128)(2,1)S(1)}, u32[]{:S(2)}, u32[]{:S(2)}) collective-permute-start(bf16[16,16,256]{2,1,0:T(8,128)(2,1)S(1)} %bitcast.200), channel_id=1, source_target_pairs={{0,16},{4,20},{8,24},{12,28},{16,0},{20,4},{24,8},{28,12},{1,17},{... | collective-permute-start | bytes 393224 | tf_op jit(solution)/shard_map/ppermute | solution.py:46
  18.9 19.2 %collective-permute-start.4 = (bf16[16,16,256]{2,1,0:T(8,128)(2,1)S(1)}, bf16[16,16,256]{2,1,0:T(8,128)(2,1)S(1)}, u32[]{:S(2)}, u32[]{:S(2)}) collective-permute-start(bf16[16,16,256]{2,1,0:T(8,128)(2,1)S(1)} %bitcast.198), channel_id=1, source_target_pairs={{0,20},{4,16},{8,28},{12,24},{16,4},{20,0},{24,12},{28,8},{1,21},{... | collective-permute-start | bytes 393224 | tf_op jit(solution)/shard_map/ppermute | solution.py:46
  20.4 17.7 %collective-permute-start.5 = (bf16[16,16,256]{2,1,0:T(8,128)(2,1)S(1)}, bf16[16,16,256]{2,1,0:T(8,128)(2,1)S(1)}, u32[]{:S(2)}, u32[]{:S(2)}) collective-permute-start(bf16[16,16,256]{2,1,0:T(8,128)(2,1)S(1)} %bitcast.202), channel_id=1, source_target_pairs={{0,24},{4,28},{8,16},{12,20},{16,8},{20,12},{24,0},{28,4},{1,25},{... | collective-permute-start | bytes 393224 | tf_op jit(solution)/shard_map/ppermute | solution.py:46
  24.6 13.5 %collective-permute-start.6 = (bf16[16,16,256]{2,1,0:T(8,128)(2,1)S(1)}, bf16[16,16,256]{2,1,0:T(8,128)(2,1)S(1)}, u32[]{:S(2)}, u32[]{:S(2)}) collective-permute-start(bf16[16,16,256]{2,1,0:T(8,128)(2,1)S(1)} %bitcast.199), channel_id=1, source_target_pairs={{0,28},{4,24},{8,20},{12,16},{16,12},{20,8},{24,4},{28,0},{1,29},{... | collective-permute-start | bytes 393224 | tf_op jit(solution)/shard_map/ppermute | solution.py:46
  41.7 12.1 %copy-start.3 = (s32[1,192]{1,0:T(1,128)S(1)}, s32[1,192]{1,0:T(1,128)}, u32[]{:S(2)}) copy-start(s32[1,192]{1,0:T(1,128)} %param.12) | copy-start | bytes 2308
  58.2 10.9 %collective-permute-start.7 = (bf16[16,16,256]{2,1,0:T(8,128)(2,1)S(1)}, bf16[16,16,256]{2,1,0:T(8,128)(2,1)S(1)}, u32[]{:S(2)}, u32[]{:S(2)}) collective-permute-start(bf16[16,16,256]{2,1,0:T(8,128)(2,1)S(1)} %bitcast.215), channel_id=1, source_target_pairs={{0,4},{4,0},{8,12},{12,8},{16,20},{20,16},{24,28},{28,24},{1,5},{5... | collective-permute-start | bytes 393224 | tf_op jit(solution)/shard_map/ppermute | solution.py:46
  59.1 12.4 %collective-permute-start.8 = (bf16[16,16,256]{2,1,0:T(8,128)(2,1)S(1)}, bf16[16,16,256]{2,1,0:T(8,128)(2,1)S(1)}, u32[]{:S(2)}, u32[]{:S(2)}) collective-permute-start(bf16[16,16,256]{2,1,0:T(8,128)(2,1)S(1)} %bitcast.213), channel_id=1, source_target_pairs={{0,8},{4,12},{8,0},{12,4},{16,24},{20,28},{24,16},{28,20},{1,9},{5... | collective-permute-start | bytes 393224 | tf_op jit(solution)/shard_map/ppermute | solution.py:46
  64.1 10.0 %collective-permute-start.9 = (bf16[16,16,256]{2,1,0:T(8,128)(2,1)S(1)}, bf16[16,16,256]{2,1,0:T(8,128)(2,1)S(1)}, u32[]{:S(2)}, u32[]{:S(2)}) collective-permute-start(bf16[16,16,256]{2,1,0:T(8,128)(2,1)S(1)} %bitcast.210), channel_id=1, source_target_pairs={{0,12},{4,8},{8,4},{12,0},{16,28},{20,24},{24,20},{28,16},{1,13},{... | collective-permute-start | bytes 393224 | tf_op jit(solution)/shard_map/ppermute | solution.py:46
  65.2 18.6 %collective-permute-start.10 = (bf16[16,16,256]{2,1,0:T(8,128)(2,1)S(1)}, bf16[16,16,256]{2,1,0:T(8,128)(2,1)S(1)}, u32[]{:S(2)}, u32[]{:S(2)}) collective-permute-start(bf16[16,16,256]{2,1,0:T(8,128)(2,1)S(1)} %bitcast.207), channel_id=1, source_target_pairs={{0,16},{4,20},{8,24},{12,28},{16,0},{20,4},{24,8},{28,12},{1,17},{... | collective-permute-start | bytes 393224 | tf_op jit(solution)/shard_map/ppermute | solution.py:46
  68.8 17.9 %collective-permute-start.11 = (bf16[16,16,256]{2,1,0:T(8,128)(2,1)S(1)}, bf16[16,16,256]{2,1,0:T(8,128)(2,1)S(1)}, u32[]{:S(2)}, u32[]{:S(2)}) collective-permute-start(bf16[16,16,256]{2,1,0:T(8,128)(2,1)S(1)} %bitcast.205), channel_id=1, source_target_pairs={{0,20},{4,16},{8,28},{12,24},{16,4},{20,0},{24,12},{28,8},{1,21},{... | collective-permute-start | bytes 393224 | tf_op jit(solution)/shard_map/ppermute | solution.py:46
  69.1 17.7 %collective-permute-start.12 = (bf16[16,16,256]{2,1,0:T(8,128)(2,1)S(1)}, bf16[16,16,256]{2,1,0:T(8,128)(2,1)S(1)}, u32[]{:S(2)}, u32[]{:S(2)}) collective-permute-start(bf16[16,16,256]{2,1,0:T(8,128)(2,1)S(1)} %bitcast.203), channel_id=1, source_target_pairs={{0,24},{4,28},{8,16},{12,20},{16,8},{20,12},{24,0},{28,4},{1,25},{... | collective-permute-start | bytes 393224 | tf_op jit(solution)/shard_map/ppermute | solution.py:46
  71.5 15.3 %collective-permute-start.13 = (bf16[16,16,256]{2,1,0:T(8,128)(2,1)S(1)}, bf16[16,16,256]{2,1,0:T(8,128)(2,1)S(1)}, u32[]{:S(2)}, u32[]{:S(2)}) collective-permute-start(bf16[16,16,256]{2,1,0:T(8,128)(2,1)S(1)} %bitcast.196), channel_id=1, source_target_pairs={{0,28},{4,24},{8,20},{12,16},{16,12},{20,8},{24,4},{28,0},{1,29},{... | collective-permute-start | bytes 393224 | tf_op jit(solution)/shard_map/ppermute | solution.py:46
  105.8 1.0 copy-start.2
  109.8 10.2 %collective-permute-start.14 = (bf16[16,16,256]{2,1,0:T(8,128)(2,1)S(1)}, bf16[16,16,256]{2,1,0:T(8,128)(2,1)S(1)}, u32[]{:S(2)}, u32[]{:S(2)}) collective-permute-start(bf16[16,16,256]{2,1,0:T(8,128)(2,1)S(1)} %bitcast.216), channel_id=1, source_target_pairs={{0,4},{4,0},{8,12},{12,8},{16,20},{20,16},{24,28},{28,24},{1,5},{5... | collective-permute-start | bytes 393224 | tf_op jit(solution)/shard_map/ppermute | solution.py:46
  111.2 11.0 %collective-permute-start.15 = (bf16[16,16,256]{2,1,0:T(8,128)(2,1)S(1)}, bf16[16,16,256]{2,1,0:T(8,128)(2,1)S(1)}, u32[]{:S(2)}, u32[]{:S(2)}) collective-permute-start(bf16[16,16,256]{2,1,0:T(8,128)(2,1)S(1)} %bitcast.214), channel_id=1, source_target_pairs={{0,8},{4,12},{8,0},{12,4},{16,24},{20,28},{24,16},{28,20},{1,9},{5... | collective-permute-start | bytes 393224 | tf_op jit(solution)/shard_map/ppermute | solution.py:46
  115.8 10.0 %collective-permute-start.16 = (bf16[16,16,256]{2,1,0:T(8,128)(2,1)S(1)}, bf16[16,16,256]{2,1,0:T(8,128)(2,1)S(1)}, u32[]{:S(2)}, u32[]{:S(2)}) collective-permute-start(bf16[16,16,256]{2,1,0:T(8,128)(2,1)S(1)} %bitcast.211), channel_id=1, source_target_pairs={{0,12},{4,8},{8,4},{12,0},{16,28},{20,24},{24,20},{28,16},{1,13},{... | collective-permute-start | bytes 393224 | tf_op jit(solution)/shard_map/ppermute | solution.py:46
  116.8 18.0 %collective-permute-start.17 = (bf16[16,16,256]{2,1,0:T(8,128)(2,1)S(1)}, bf16[16,16,256]{2,1,0:T(8,128)(2,1)S(1)}, u32[]{:S(2)}, u32[]{:S(2)}) collective-permute-start(bf16[16,16,256]{2,1,0:T(8,128)(2,1)S(1)} %bitcast.208), channel_id=1, source_target_pairs={{0,16},{4,20},{8,24},{12,28},{16,0},{20,4},{24,8},{28,12},{1,17},{... | collective-permute-start | bytes 393224 | tf_op jit(solution)/shard_map/ppermute | solution.py:46
  119.0 18.4 %collective-permute-start.18 = (bf16[16,16,256]{2,1,0:T(8,128)(2,1)S(1)}, bf16[16,16,256]{2,1,0:T(8,128)(2,1)S(1)}, u32[]{:S(2)}, u32[]{:S(2)}) collective-permute-start(bf16[16,16,256]{2,1,0:T(8,128)(2,1)S(1)} %bitcast.206), channel_id=1, source_target_pairs={{0,20},{4,16},{8,28},{12,24},{16,4},{20,0},{24,12},{28,8},{1,21},{... | collective-permute-start | bytes 393224 | tf_op jit(solution)/shard_map/ppermute | solution.py:46
  120.1 17.4 %collective-permute-start.19 = (bf16[16,16,256]{2,1,0:T(8,128)(2,1)S(1)}, bf16[16,16,256]{2,1,0:T(8,128)(2,1)S(1)}, u32[]{:S(2)}, u32[]{:S(2)}) collective-permute-start(bf16[16,16,256]{2,1,0:T(8,128)(2,1)S(1)} %bitcast.204), channel_id=1, source_target_pairs={{0,24},{4,28},{8,16},{12,20},{16,8},{20,12},{24,0},{28,4},{1,25},{... | collective-permute-start | bytes 393224 | tf_op jit(solution)/shard_map/ppermute | solution.py:46
  122.2 15.3 %collective-permute-start.20 = (bf16[16,16,256]{2,1,0:T(8,128)(2,1)S(1)}, bf16[16,16,256]{2,1,0:T(8,128)(2,1)S(1)}, u32[]{:S(2)}, u32[]{:S(2)}) collective-permute-start(bf16[16,16,256]{2,1,0:T(8,128)(2,1)S(1)} %bitcast.197), channel_id=1, source_target_pairs={{0,28},{4,24},{8,20},{12,16},{16,12},{20,8},{24,4},{28,0},{1,29},{... | collective-permute-start | bytes 393224 | tf_op jit(solution)/shard_map/ppermute | solution.py:46
  156.7 2.6 %copy-start.1 = (bf16[64,16384]{1,0:T(8,128)(2,1)S(1)}, bf16[64,16384]{1,0:T(8,128)(2,1)}, u32[]{:S(2)}) copy-start(bf16[64,16384]{1,0:T(8,128)(2,1)} %all-gather.2.cloned.1.call-done) | copy-start | bytes 6291460
Sparse Core Ops, SparseCore 0:
  107.8 25.0 all-gather.1
